TPU v7x, 512 devices: a whole 4x8x8 slice. The times are simulated.
512 devices in a mesh: section: 2 (over core), req: 64 (over y, z), head: 4 (over x).
Axes of the slice: x: 4, y: 8, z: 8, core: 2. Of those that a mesh axis runs over, the one named last changes fastest.
Arguments:
- embedding_per_slot: bfloat16 [512, 4, 1024], P('req', None, 'head'), may hold values from -6 to 6
- tally_per_slot: int32 [512], P('req'), may hold values from 1 to 4
- slot_requests: int32 [512], replicated, may hold values from 0 to 511, as said below
- memory_per_request: float32 [2, 512, 16, 64, 64], P('section', 'req', 'head'), may hold values from -4 to 4
- previous_step_feature: bfloat16 [2, 512, 1024], P('section', 'req', 'head'), may hold values from -6 to 6
- lag_interpolants: bfloat16 [2, 5, 1024], P('section'), may hold values from 0 to 1
- acceptor_projection: bfloat16 [2, 1024, 1024], P('section', None, 'head'), may hold values from -0.1875 to 0.1875
- address_projection: bfloat16 [2, 1024, 1024], P('section', None, 'head'), may hold values from -0.1875 to 0.1875
- content_projection: bfloat16 [2, 1024, 1024], P('section', None, 'head'), may hold values from -0.1875 to 0.1875
- readout_projection: bfloat16 [2, 1024, 1024], P('section', 'head'), may hold values from -0.1875 to 0.1875
- fading_first_lowrank: bfloat16 [2, 1024, 96], P('section', 'head'), may hold values from -0.1875 to 0.1875
- fading_second_lowrank: bfloat16 [2, 96, 1024], P('section', None, 'head'), may hold values from -0.625 to 0.625
- adapt_first_lowrank: bfloat16 [2, 1024, 96], P('section', 'head'), may hold values from -0.1875 to 0.1875
- adapt_second_lowrank: bfloat16 [2, 96, 1024], P('section', None, 'head'), may hold values from -0.625 to 0.625
- fading_baseline: float32 [2, 1024], P('section', 'head'), may hold values from -4 to 1
- adapt_baseline: float32 [2, 1024], P('section', 'head'), may hold values from -3 to 3
- erasing_address_gains: float32 [2, 1024], P('section', 'head'), may hold values from 0.5 to 1.5
- address_rate_coupling: float32 [2, 1024], P('section', 'head'), may hold values from 0 to 1
- present_extra_gain: float32 [2, 1024], P('section', 'head'), may hold values from -3 to 3
- section_standard_gains: float32 [2, 1024], P('section', 'head'), may hold values from 0.1 to 1.9
- section_standard_shift_terms: float32 [2, 1024], P('section', 'head'), may hold values from -2 to 2
Outputs:
- layer_out: bfloat16 [2, 512, 4, 1024], P('section', 'req', None, 'head')
Inputs may be any that keep to these rules, and one draw needn't show every extreme that they name: `slot_requests`: every request appears once. Of one group's 8 arrival slots at most 1 hold requests stored in any one group, and each group holds exactly 1 from some group.
All inputs are finite; a program needn't handle non-finite values.
Results may differ from a plain program's by a relative error of at most 0.02.
Values may be sent and summed in bfloat16 or wider, within the bound.
No kernel may reach another device: no remote copies, remote signals or barrier semaphores. Data moves between devices by JAX's collectives and lax.ppermute only.
A program may use at most 64 MiB of HBM per device.

v0:
```python
import jax
import jax.numpy as jnp
from jax import lax
from jax.sharding import PartitionSpec as P

highest = lax.Precision.HIGHEST


def from_behind(block, axis, distance):
    devices = range(lax.axis_size(axis))
    route = [(i - distance, i) for i in devices if i - distance in devices]
    return lax.ppermute(block, axis, route)


def sequence_recurrence(
    acceptor_entries,
    address_entries,
    content_entries,
    latent_response,
    adapt_latent,
    starting_memory,
    fading_second_lowrank,
    adapt_second_lowrank,
    fading_baseline,
    adapt_baseline,
    erasing_address_gains,
    address_rate_coupling,
    present_extra_gain,
    section_standard_gains,
    section_standard_shift_terms,
):
    batch_rows = starting_memory.shape[0]
    stored_memory_parts = starting_memory.shape[1]
    subspace_span = starting_memory.shape[2]

    def to_heads(array_in):
        return array_in.reshape(batch_rows, -1, stored_memory_parts, subspace_span)

    log_rate = (
        -jax.nn.softplus(
            -(
                fading_baseline
                + jnp.dot(
                    latent_response, fading_second_lowrank, preferred_element_type=jnp.float32
                )
            )
        )
        - 0.5
    )
    decays = to_heads(jnp.exp(-jnp.exp(log_rate)))
    learning = jax.nn.sigmoid(
        adapt_baseline
        + jnp.dot(adapt_latent, adapt_second_lowrank, preferred_element_type=jnp.float32)
    )
    learn_heads = to_heads(learning)
    scaled = to_heads(address_entries * erasing_address_gains)
    normed = scaled / jnp.sqrt(jnp.sum(scaled * scaled, axis=-1, keepdims=True) + 1e-06)
    erasing_address = to_heads(address_entries * (1.0 + (learning - 1.0) * address_rate_coupling))
    acceptor_parts = to_heads(acceptor_entries)
    content_part_lines = to_heads(content_entries)
    states = starting_memory
    readout = []
    for position in range(acceptor_parts.shape[1]):
        pulled = jnp.einsum("rhij,rhj->rhi", states, normed[:, position], precision=highest)
        states = (
            states * decays[:, position][:, :, None, :]
            - jnp.einsum(
                "rhi,rhj->rhij",
                pulled,
                normed[:, position] * learn_heads[:, position],
                precision=highest,
            )
            + jnp.einsum(
                "rhi,rhj->rhij",
                content_part_lines[:, position],
                erasing_address[:, position],
                precision=highest,
            )
        )
        readout.append(
            jnp.einsum("rhij,rhj->rhi", states, acceptor_parts[:, position], precision=highest)
        )
    read_all = jnp.stack(readout, axis=1)
    center = read_all - jnp.mean(read_all, axis=-1, keepdims=True)
    variance = jnp.mean(center * center, axis=-1, keepdims=True)
    gain_heads = section_standard_gains.reshape(stored_memory_parts, subspace_span)
    bias_heads = section_standard_shift_terms.reshape(stored_memory_parts, subspace_span)
    standardized_parts = center / jnp.sqrt(variance + 0.00064) * gain_heads + bias_heads
    present_extra_term = (
        jnp.sum(
            acceptor_parts
            * erasing_address
            * present_extra_gain.reshape(stored_memory_parts, subspace_span),
            axis=-1,
            keepdims=True,
        )
        * content_part_lines
    )
    return (
        (standardized_parts + present_extra_term)
        .astype(jnp.bfloat16)
        .reshape(-1, stored_memory_parts * subspace_span)
    )


def run_sublevel(lowrank_latent, earlier_entry, starting_memory, params):
    (
        lag_interpolants,
        acceptor_projection,
        address_projection,
        content_projection,
        readout_projection,
        fading_first_lowrank,
        fading_second_lowrank,
        adapt_first_lowrank,
        adapt_second_lowrank,
        fading_baseline,
        adapt_baseline,
        erasing_address_gains,
        address_rate_coupling,
        present_extra_gain,
        section_standard_gains,
        section_standard_shift_terms,
    ) = params
    batch_rows, steps_count, shard_width = lowrank_latent.shape
    previous = jnp.concatenate([earlier_entry[:, None, :], lowrank_latent[:, :-1, :]], axis=1)
    piece_now = lax.all_gather(lowrank_latent, "head", axis=2, tiled=True)
    piece_prev = lax.all_gather(previous, "head", axis=2, tiled=True)
    span_width = piece_now.shape[2]
    coef_rows = lag_interpolants.astype(jnp.float32)
    current_piece = piece_now.astype(jnp.float32)
    spread_piece = piece_prev.astype(jnp.float32) - current_piece
    updated = []
    for slot_num, which_mix, weight_all in (
        (0, 0, acceptor_projection),
        (1, 2, address_projection),
        (2, 3, content_projection),
    ):
        blend = (
            (current_piece + spread_piece * coef_rows[which_mix])
            .astype(jnp.bfloat16)
            .reshape(-1, span_width)
        )
        updated.append(jnp.dot(blend, weight_all, preferred_element_type=jnp.float32))
    acceptor_entries = updated[0]
    address_entries = updated[1]
    content_entries = updated[2]
    current = lowrank_latent.astype(jnp.float32)
    spread = previous.astype(jnp.float32) - current
    column_start = lax.axis_index("head") * shard_width
    decay_mix = lax.dynamic_slice_in_dim(lag_interpolants[1], column_start, shard_width, 0).astype(
        jnp.float32
    )
    learn_mix = lax.dynamic_slice_in_dim(lag_interpolants[4], column_start, shard_width, 0).astype(
        jnp.float32
    )
    decay_input = (current + spread * decay_mix).astype(jnp.bfloat16).reshape(-1, shard_width)
    learn_input = (current + spread * learn_mix).astype(jnp.bfloat16).reshape(-1, shard_width)
    partial_rank = jnp.dot(decay_input, fading_first_lowrank, preferred_element_type=jnp.float32)
    partial_learn = jnp.dot(learn_input, adapt_first_lowrank, preferred_element_type=jnp.float32)
    decay_total, learn_total = lax.psum((partial_rank, partial_learn), "head")
    latent_response = jnp.tanh(decay_total).astype(jnp.bfloat16)
    adapt_latent = learn_total.astype(jnp.bfloat16)
    lagged_features = sequence_recurrence(
        acceptor_entries,
        address_entries,
        content_entries,
        latent_response,
        adapt_latent,
        starting_memory,
        fading_second_lowrank,
        adapt_second_lowrank,
        fading_baseline,
        adapt_baseline,
        erasing_address_gains,
        address_rate_coupling,
        present_extra_gain,
        section_standard_gains,
        section_standard_shift_terms,
    )
    own_rows = lax.psum_scatter(
        lax.dot_general(
            readout_projection,
            lagged_features,
            (((0,), (1,)), ((), ())),
            preferred_element_type=jnp.float32,
        ),
        "head",
        scatter_dimension=0,
        tiled=True,
    )
    projected = own_rows.T.reshape(batch_rows, steps_count, shard_width)
    return (current + projected).astype(jnp.bfloat16)


def run_sections(inputs, states_use, last_use, params):
    section_num = lax.axis_index("section")
    section_count = lax.axis_size("section")
    block_count = 1
    block_rows = inputs.shape[0] // block_count
    result = jnp.zeros_like(inputs)
    incoming = jnp.zeros((block_rows,) + inputs.shape[1:], jnp.bfloat16)
    tick_total = block_count + section_count - 1
    for tick_num in range(tick_total):
        lag = tick_num - section_num
        entering = jnp.where(section_num == 0, inputs, incoming)
        produced = run_sublevel(entering, last_use, states_use, params)
        is_valid = (lag >= 0) & (lag < block_count)
        result = jnp.where(is_valid, produced, result)
        if tick_num + 1 < tick_total:
            incoming = from_behind(produced, "section", 1)
    return result


def body(
    embedding_per_slot,
    tally_per_slot,
    slot_requests,
    memory_per_request,
    previous_step_feature,
    lag_interpolants,
    acceptor_projection,
    address_projection,
    content_projection,
    readout_projection,
    fading_first_lowrank,
    fading_second_lowrank,
    adapt_first_lowrank,
    adapt_second_lowrank,
    fading_baseline,
    adapt_baseline,
    erasing_address_gains,
    address_rate_coupling,
    present_extra_gain,
    section_standard_gains,
    section_standard_shift_terms,
):
    local_rows = embedding_per_slot.shape[0]
    groups = lax.axis_size("req")
    capacity = (local_rows + groups - 1) // groups
    my_group = lax.axis_index("req")
    slot_ids = jnp.arange(local_rows, dtype=jnp.int32)
    table = slot_requests.reshape(groups, local_rows)
    my_arrivals = lax.dynamic_index_in_dim(table, my_group, 0, keepdims=False)
    home_group = my_arrivals // local_rows
    earlier = slot_ids[None, :] < slot_ids[:, None]
    arrival_rank = jnp.sum(
        ((home_group[:, None] == home_group[None, :]) & earlier).astype(jnp.int32), axis=1
    )
    arrival_slot = home_group * capacity + arrival_rank
    requests = my_group * local_rows + slot_ids
    total_rows = slot_requests.shape[0]
    found = slot_requests[None, :] == requests[:, None]
    positions = jnp.sum(
        jnp.where(found, jnp.arange(total_rows, dtype=jnp.int32)[None, :], 0), axis=1
    )
    source = positions // local_rows
    within = positions % local_rows
    source_homes = jnp.take(table, source, axis=0) // local_rows
    home_rank = jnp.sum(
        ((source_homes == my_group) & (slot_ids[None, :] < within[:, None])).astype(jnp.int32),
        axis=1,
    )
    home_slot = source * capacity + home_rank
    buffer_rows = groups * capacity
    params = (
        lag_interpolants[0],
        acceptor_projection[0],
        address_projection[0],
        content_projection[0],
        readout_projection[0],
        fading_first_lowrank[0],
        fading_second_lowrank[0],
        adapt_first_lowrank[0],
        adapt_second_lowrank[0],
        fading_baseline[0],
        adapt_baseline[0],
        erasing_address_gains[0],
        address_rate_coupling[0],
        present_extra_gain[0],
        section_standard_gains[0],
        section_standard_shift_terms[0],
    )
    states_local = memory_per_request[0]
    last_local = previous_step_feature[0]
    outgoing = (
        jnp.zeros((buffer_rows,) + embedding_per_slot.shape[1:], jnp.bfloat16)
        .at[arrival_slot]
        .set(embedding_per_slot)
    )
    arrived = lax.all_to_all(outgoing, "req", split_axis=0, concat_axis=0, tiled=True)
    inputs = jnp.take(arrived, home_slot, axis=0)
    result = run_sections(inputs, states_local, last_local, params)
    going_back = (
        jnp.zeros((buffer_rows,) + result.shape[1:], jnp.bfloat16).at[home_slot].set(result)
    )
    returned = lax.all_to_all(going_back, "req", split_axis=0, concat_axis=0, tiled=True)
    result = jnp.take(returned, arrival_slot, axis=0)
    live_mask = (
        jnp.arange(embedding_per_slot.shape[1], dtype=jnp.int32)[None, :] < tally_per_slot[:, None]
    )
    return jnp.where(live_mask[:, :, None], result, jnp.zeros_like(result))[None]


def solution(mesh):
    return jax.shard_map(
        body,
        mesh=mesh,
        in_specs=(
            P("req", None, "head"),
            P("req"),
            P(),
            P("section", "req", "head", None, None),
            P("section", "req", "head"),
            P("section", None, None),
            P("section", None, "head"),
            P("section", None, "head"),
            P("section", None, "head"),
            P("section", "head", None),
            P("section", "head", None),
            P("section", None, "head"),
            P("section", "head", None),
            P("section", None, "head"),
            P("section", "head"),
            P("section", "head"),
            P("section", "head"),
            P("section", "head"),
            P("section", "head"),
            P("section", "head"),
            P("section", "head"),
        ),
        out_specs=P("section", "req", None, "head"),
        check_vma=False,
    )
```

profile of v0, /device:TPU:8, one launch (start us, length us, event | category | flops | bytes accessed | tf_op | source)
XLA Modules:
  0.0 273.9 jit_solution(2103046319629629872)
XLA Ops:
  6.5 0.9 reshape.364
  7.7 0.7 broadcast.410.clone
  8.4 2.0 scatter_fusion
  10.3 16.6 %all-to-all-start = ((bf16[64,4,256]{2,1,0:T(4,128)(2,1)}), bf16[64,4,256]{2,1,0:T(4,128)(2,1)S(1)}, u32[]{:S(2)}, u32[]{:S(2)}) async-start(bf16[64,4,256]{2,1,0:T(4,128)(2,1)} %scatter_fusion), calls=%async_computation | async-start | bytes 262144 | tf_op jit(solution)/shard_map/all_to_all | solution.py:291
  27.0 0.9 select_reduce_fusion
  30.0 0.8 copy-done.4
  31.7 0.7 reduce.9
  33.1 0.7 reduce.10
  33.8 0.7 mul.345
  34.4 0.7 reduce.11
  35.1 0.7 mul.349
  36.4 2.2 all-to-all-done
  39.2 12.3 %all_gather.12 = bf16[8,4,1024]{2,0,1:T(8,128)(2,1)S(1)} all-gather(bf16[8,4,256]{2,0,1:T(8,128)(2,1)S(1)} %broadcast_select_fusion.1), channel_id=1, replica_groups=mesh['section'=2,'req'=64,'head'=4] {'head'}, dimensions={2}, use_global_device_ids=true | all-gather | bytes 81920 | tf_op jit(solution)/shard_map/all_gather | solution.py:127
  51.5 11.9 %all_gather.13 = bf16[8,4,1024]{2,0,1:T(8,128)(2,1)S(1)} all-gather(bf16[8,4,256]{2,0,1:T(8,128)(2,1)S(1)} %pad_maximum_fusion.3), channel_id=1, replica_groups=mesh['section'=2,'req'=64,'head'=4] {'head'}, dimensions={2}, use_global_device_ids=true | all-gather | bytes 81920 | tf_op jit(solution)/shard_map/all_gather | solution.py:128
  63.7 0.7 copy-done.5
  64.6 0.7 copy-done.6
  65.4 16.7 %all-reduce.1 = (bf16[32,96]{1,0:T(8,128)(2,1)S(1)}, f32[32,96]{1,0:T(8,128)S(1)}) all-reduce(f32[32,96]{1,0:T(8,128)S(1)} %fusion.86, f32[32,96]{1,0:T(8,128)S(1)} %fusion.92), channel_id=1, replica_groups=mesh['section'=2,'req'=64,'head'=4] {'head'}, use_global_device_ids=true, to_apply=%region_6.8 | all-reduce | flops 6144 | bytes 43008 | tf_op jit(solution)/shard_map/psum | solution.py:161
  87.3 0.7 copy-done.60
  88.0 1.6 fusion.104
  89.5 0.8 reshape.366
  90.4 0.7 copy-done.19
  91.5 0.7 copy-done.13
  92.2 1.7 fusion.20
  93.9 2.1 fusion.137
  96.0 0.7 copy-done.30
  96.7 2.1 fusion.160
  98.8 0.7 copy-done.9
  99.6 3.2 %fusion.55 = f32[8,4,1,64]{3,2,1,0:T(1,128)S(1)} fusion(f32[8,4,64]{2,1,0:T(4,128)S(1)} %copy-done.15, f32[8,4,64]{2,1,0:T(4,128)S(1)} %copy.164, f32[8,4,64]{2,1,0:T(4,128)S(1)} %copy-done.9, f32[8,4,64]{2,1,0:T(4,128)S(1)} %bitcast.461, f32[8,4,64]{2,1,0:T(4,128)S(1)} %get-tuple-element.50, f32[8,4,64,1]{2,0,1,3:T(8,128)S(1)} %copy-done.31, ...), kind=kOutput, calls=%fused_computation.72 | convolution fusion | flops 2883584 | bytes 622592 | tf_op jit(solution)/shard_map/rhij,rhj->rhi/dot_general | solution.py:81
  102.8 0.7 copy-done.29
  103.5 2.8 %fusion.54 = f32[8,4,1,64]{3,2,1,0:T(1,128)S(1)} fusion(f32[8,4,64,1]{2,3,1,0:T(1,128)S(1)} %bitcast.471, f32[8,4,64]{2,1,0:T(4,128)S(1)} %copy-done.15, f32[8,4,64]{2,1,0:T(4,128)S(1)} %copy.164, f32[8,4,64]{2,1,0:T(4,128)S(1)} %copy-done.9, f32[8,4,64]{2,1,0:T(4,128)S(1)} %bitcast.462, f32[8,4,64]{2,1,0:T(4,128)S(1)} %get-tuple-element.50, ...), kind=kOutput, calls=%fused_computation.71 | convolution fusion | flops 2883584 | bytes 622592 | tf_op jit(solution)/shard_map/rhij,rhj->rhi/dot_general | solution.py:64
  106.3 0.7 copy-done.14
  107.0 2.0 multiply_add_fusion.2
  109.1 1.7 fusion.134
  110.8 0.7 copy-done.11
  111.5 1.7 fusion.168
  113.3 0.7 copy-done.26
  114.0 2.1 fusion.32
  117.5 0.9 convolution_bitcast_fusion.1
  118.4 22.9 %reduce-scatter.3.cloned.1.call-done = f32[256,32]{0,1:T(8,128)} async-done(((f32[1024,32]{0,1:T(8,128)}), f32[256,32]{0,1:T(8,128)}) %reduce-scatter.3.cloned.1.call-update) | async-done | bytes 32784 | tf_op jit(solution)/shard_map/reduce_scatter | solution.py:181
  141.3 0.8 reshape.373
  142.1 1.3 collective-permute-start
  143.4 0.8 collective-permute-done
  144.3 12.0 %all_gather.14 = bf16[8,4,1024]{2,0,1:T(8,128)(2,1)S(1)} all-gather(bf16[8,4,256]{2,0,1:T(8,128)(2,1)S(1)} %broadcast_select_fusion), channel_id=1, replica_groups=mesh['section'=2,'req'=64,'head'=4] {'head'}, dimensions={2}, use_global_device_ids=true | all-gather | bytes 81920 | tf_op jit(solution)/shard_map/all_gather | solution.py:127
  156.4 11.9 %all_gather.15 = bf16[8,4,1024]{2,0,1:T(8,128)(2,1)S(1)} all-gather(bf16[8,4,256]{2,0,1:T(8,128)(2,1)S(1)} %pad_maximum_fusion.2), channel_id=1, replica_groups=mesh['section'=2,'req'=64,'head'=4] {'head'}, dimensions={2}, use_global_device_ids=true | all-gather | bytes 81920 | tf_op jit(solution)/shard_map/all_gather | solution.py:128
  170.9 0.8 copy-done.7
  171.8 15.1 %all-reduce = (bf16[32,96]{1,0:T(8,128)(2,1)S(1)}, f32[32,96]{1,0:T(8,128)S(1)}) all-reduce(f32[32,96]{1,0:T(8,128)S(1)} %fusion.84, f32[32,96]{1,0:T(8,128)S(1)} %fusion.90), channel_id=1, replica_groups=mesh['section'=2,'req'=64,'head'=4] {'head'}, use_global_device_ids=true, to_apply=%region_13.15 | all-reduce | flops 6144 | bytes 43008 | tf_op jit(solution)/shard_map/psum | solution.py:161
  189.1 1.7 fusion.18
  191.0 0.8 copy-done.57
  192.1 2.1 fusion.131
  194.1 2.1 fusion.155
  196.2 3.2 %fusion.57 = f32[8,4,1,64]{3,2,1,0:T(1,128)S(1)} fusion(f32[8,4,64]{2,1,0:T(4,128)S(1)} %get-tuple-element.42, f32[8,4,64]{2,1,0:T(4,128)S(1)} %copy.178, f32[8,4,64]{2,1,0:T(4,128)S(1)} %get-tuple-element.18, f32[8,4,64]{2,1,0:T(4,128)S(1)} %bitcast.464, f32[8,4,64]{2,1,0:T(4,128)S(1)} %get-tuple-element.30, f32[8,4,64,1]{2,0,1,3:T(8,128)S(1)} %get-tuple-element.27, ...), kind=kOutput, calls=%fused_computation.74 | convolution fusion | flops 2883584 | bytes 622592 | tf_op jit(solution)/shard_map/rhij,rhj->rhi/dot_general | solution.py:81
  199.5 2.8 %fusion.56 = f32[8,4,1,64]{3,2,1,0:T(1,128)S(1)} fusion(f32[8,4,64,1]{2,3,1,0:T(1,128)S(1)} %bitcast.473, f32[8,4,64]{2,1,0:T(4,128)S(1)} %get-tuple-element.42, f32[8,4,64]{2,1,0:T(4,128)S(1)} %copy.178, f32[8,4,64]{2,1,0:T(4,128)S(1)} %get-tuple-element.18, f32[8,4,64]{2,1,0:T(4,128)S(1)} %bitcast.465, f32[8,4,64]{2,1,0:T(4,128)S(1)} %get-tuple-element.30, ...), kind=kOutput, calls=%fused_computation.73 | convolution fusion | flops 2883584 | bytes 622592 | tf_op jit(solution)/shard_map/rhij,rhj->rhi/dot_general | solution.py:64
  202.3 2.0 multiply_add_fusion
  204.3 1.7 fusion.128
  206.1 1.7 fusion.169
  207.8 2.1 fusion.26
  210.7 0.9 convolution_bitcast_fusion
  212.9 0.7 compare_and_fusion
  213.6 23.6 %reduce-scatter.5.cloned.1.call-done = f32[256,32]{0,1:T(8,128)} async-done(((f32[1024,32]{0,1:T(8,128)}), f32[256,32]{0,1:T(8,128)}) %reduce-scatter.5.cloned.1.call-update) | async-done | bytes 32784 | tf_op jit(solution)/shard_map/reduce_scatter | solution.py:181
  237.2 0.8 reshape.382
  238.0 0.7 broadcast.410
  238.7 1.9 scatter_fusion.1
  240.6 13.4 %all-to-all-start.1 = ((bf16[64,4,256]{2,1,0:T(4,128)(2,1)}), bf16[64,4,256]{2,1,0:T(4,128)(2,1)S(1)}, u32[]{:S(2)}, u32[]{:S(2)}) async-start(bf16[64,4,256]{2,1,0:T(4,128)(2,1)} %scatter_fusion.1), calls=%async_computation.3 | async-start | bytes 262144 | tf_op jit(solution)/shard_map/all_to_all | solution.py:297
  254.7 11.1 %all-to-all-done.1 = bf16[64,4,256]{2,1,0:T(4,128)(2,1)S(1)} async-done(((bf16[64,4,256]{2,1,0:T(4,128)(2,1)}), bf16[64,4,256]{2,1,0:T(4,128)(2,1)S(1)}, u32[]{:S(2)}, u32[]{:S(2)}) %all-to-all-start.1) | async-done | bytes 131104 | tf_op jit(solution)/shard_map/all_to_all | solution.py:297
  (236 shorter events, 22.1 us)
Async XLA Ops:
  6.5 111.0 %copy-start = (bf16[1,256,1024]{2,1,0:T(8,128)(2,1)S(1)}, bf16[1,256,1024]{2,1,0:T(8,128)(2,1)}, u32[]{:S(2)}) copy-start(bf16[1,256,1024]{2,1,0:T(8,128)(2,1)} %param.32) | copy-start | bytes 1572868
  6.5 23.3 %copy-start.3 = (bf16[1,1024,256]{2,1,0:T(8,128)(2,1)S(1)}, bf16[1,1024,256]{2,1,0:T(8,128)(2,1)}, u32[]{:S(2)}) copy-start(bf16[1,1024,256]{2,1,0:T(8,128)(2,1)} %param.29) | copy-start | bytes 1572868
  7.4 20.9 %copy-start.8 = (s32[64,8]{1,0:T(8,128)}, s32[64,8]{1,0:T(8,128)S(1)}, u32[]{:S(2)}) copy-start(s32[64,8]{1,0:T(8,128)S(1)} %reshape.364) | copy-start | bytes 6148
  7.6 0.7 copy-start.46
  10.3 28.2 %all-to-all-start = ((bf16[64,4,256]{2,1,0:T(4,128)(2,1)}), bf16[64,4,256]{2,1,0:T(4,128)(2,1)S(1)}, u32[]{:S(2)}, u32[]{:S(2)}) async-start(bf16[64,4,256]{2,1,0:T(4,128)(2,1)} %scatter_fusion), calls=%async_computation | async-start | bytes 262144 | tf_op jit(solution)/shard_map/all_to_all | solution.py:291
  26.9 114.4 %reduce-scatter.3.cloned.1.call-start = ((), (), s32[]{:S(2)}) async-start(), calls=%async_computation.4 | async-start | bytes 163840 | tf_op jit(solution)/shard_map/reduce_scatter | solution.py:181
  28.9 0.8 copy-start.25
  29.7 33.8 %copy-start.33 = (pred[8]{0:T(512)(128)(4,1)}, pred[8]{0:T(512)(128)(4,1)S(1)}, u32[]{:S(2)}) copy-start(pred[8]{0:T(512)(128)(4,1)S(1)} %get-tuple-element.12) | copy-start | bytes 28
  29.8 33.8 %copy-start.35 = (f32[1,1,256]{2,1,0:T(1,128)}, f32[1,1,256]{2,1,0:T(1,128)S(1)}, u32[]{:S(2)}) copy-start(f32[1,1,256]{2,1,0:T(1,128)S(1)} %get-tuple-element.77) | copy-start | bytes 3076
  29.8 33.8 %copy-start.37 = (f32[1,1,256]{2,1,0:T(1,128)}, f32[1,1,256]{2,1,0:T(1,128)S(1)}, u32[]{:S(2)}) copy-start(f32[1,1,256]{2,1,0:T(1,128)S(1)} %get-tuple-element.78) | copy-start | bytes 3076
  29.8 1.0 copy-start.4
  31.1 0.7 copy-start.50
  32.4 0.7 copy-start.51
  33.8 0.7 copy-start.52
  36.4 27.0 %copy-start.23 = (f32[1,1,1024]{2,1,0:T(1,128)}, f32[1,1,1024]{2,1,0:T(1,128)S(1)}, u32[]{:S(2)}) copy-start(f32[1,1,1024]{2,1,0:T(1,128)S(1)} %get-tuple-element.73) | copy-start | bytes 12292
  36.4 49.2 %copy-start.21 = (f32[1,1,1024]{2,1,0:T(1,128)}, f32[1,1,1024]{2,1,0:T(1,128)S(1)}, u32[]{:S(2)}) copy-start(f32[1,1,1024]{2,1,0:T(1,128)S(1)} %get-tuple-element.72) | copy-start | bytes 12292
  39.2 12.3 %copy-start.17 = (bf16[1,8,256]{2,1,0:T(8,128)(2,1)S(1)}, bf16[1,8,256]{2,1,0:T(8,128)(2,1)}, u32[]{:S(2)}) copy-start(bf16[1,8,256]{2,1,0:T(8,128)(2,1)} %param.27) | copy-start | bytes 12292
  63.4 19.7 %copy-start.2 = (bf16[1,1024,256]{2,1,0:T(8,128)(2,1)S(1)}, bf16[1,1024,256]{2,1,0:T(8,128)(2,1)}, u32[]{:S(2)}) copy-start(bf16[1,1024,256]{2,1,0:T(8,128)(2,1)} %param.30) | copy-start | bytes 1572868
  63.6 0.8 copy-start.5
  64.5 0.8 copy-start.6
  65.2 16.9 %copy-start.55 = (bf16[1,96,256]{2,1,0:T(8,128)(2,1)S(1)}, bf16[1,96,256]{2,1,0:T(8,128)(2,1)}, u32[]{:S(2)}) copy-start(bf16[1,96,256]{2,1,0:T(8,128)(2,1)} %param.36) | copy-start | bytes 147460
  82.1 0.7 copy-start.58
  82.9 0.7 copy-start.41
  83.1 0.7 copy-start.39
  85.6 5.9 %copy-start.1 = (f32[1,8,4,64,64]{4,3,2,1,0:T(8,128)S(1)}, f32[1,8,4,64,64]{4,3,2,1,0:T(8,128)}, u32[]{:S(2)}) copy-start(f32[1,8,4,64,64]{4,3,2,1,0:T(8,128)} %param.26) | copy-start | bytes 1572868
  87.3 0.7 copy-start.60
  90.4 0.7 copy-start.19
  91.4 0.7 copy-start.13
  92.2 1.7 copy-start.10
  92.2 1.7 copy-start.16
  92.2 1.8 copy-start.32
  96.0 0.7 copy-start.30
  96.7 2.1 copy-start.31
  98.8 0.7 copy-start.9
  98.8 0.7 copy-start.15
  102.8 0.7 copy-start.29
  106.3 0.7 copy-start.14
  107.0 2.0 copy-start.12
  110.8 0.7 copy-start.11
  111.5 1.8 copy-start.28
  113.2 0.7 copy-start.26
  113.2 0.7 copy-start.27
  116.4 0.7 copy-start.43
  116.4 0.7 copy-start.44
  116.4 0.7 copy-start.45
  118.4 118.8 %reduce-scatter.5.cloned.1.call-start = ((), (), s32[]{:S(2)}) async-start(), calls=%async_computation.5 | async-start | bytes 163840 | tf_op jit(solution)/shard_map/reduce_scatter | solution.py:181
  141.3 0.8 copy-start.34
  142.1 2.1 collective-permute-start
  144.3 12.0 %copy-start.18 = (bf16[1,8,256]{2,1,0:T(8,128)(2,1)S(1)}, bf16[1,8,256]{2,1,0:T(8,128)(2,1)}, u32[]{:S(2)}) copy-start(bf16[1,8,256]{2,1,0:T(8,128)(2,1)} %param.27) | copy-start | bytes 12292
  156.4 11.9 %copy-start.22 = (f32[1,1,1024]{2,1,0:T(1,128)S(1)}, f32[1,1,1024]{2,1,0:T(1,128)}, u32[]{:S(2)}) copy-start(f32[1,1,1024]{2,1,0:T(1,128)} %copy-done.21) | copy-start | bytes 12292
  168.2 0.7 copy-start.24
  168.9 0.7 copy-start.38
  169.6 0.7 copy-start.20
  170.9 0.8 copy-start.7
  171.7 15.3 %copy-start.56 = (bf16[1,96,256]{2,1,0:T(8,128)(2,1)S(1)}, bf16[1,96,256]{2,1,0:T(8,128)(2,1)}, u32[]{:S(2)}) copy-start(bf16[1,96,256]{2,1,0:T(8,128)(2,1)} %param.36) | copy-start | bytes 147460
  187.0 0.7 copy-start.59
  187.8 0.7 copy-start.40
  187.8 0.7 copy-start.42
  190.9 0.8 copy-start.57
  191.0 0.8 copy-start.61
  211.5 0.7 copy-start.49
  211.5 0.7 copy-start.54
  212.2 0.7 copy-start.47
  240.6 25.1 %all-to-all-start.1 = ((bf16[64,4,256]{2,1,0:T(4,128)(2,1)}), bf16[64,4,256]{2,1,0:T(4,128)(2,1)S(1)}, u32[]{:S(2)}, u32[]{:S(2)}) async-start(bf16[64,4,256]{2,1,0:T(4,128)(2,1)} %scatter_fusion.1), calls=%async_computation.3 | async-start | bytes 262144 | tf_op jit(solution)/shard_map/all_to_all | solution.py:297
  (4 other events, 2.4 us)
Sparse Core Ops, SparseCore 0:
  118.5 22.7 reduce-scatter.2
  211.7 25.4 reduce-scatter.4
where the time goes:
time: 276 us; the launch traced here: 274 us
  blocking collectives  80 us (29%)
  waiting for transfers between devices  60.6 us (22%)
  matrix products  40.9 us (15%)
  local copies, waits for them, and re-layouts  35.8 us (13%)
  starting transfers between devices  31.3 us (11%)
  between operations  14.4 us (5%)
  other arithmetic  11 us (4%)
    reduce_scatter x2, waiting for transfers between devices, run_sublevel(): lax.psum_scatter(lax.dot_general(readout_projection, lagged_features, (((...  46.5 us
    psum x2, blocking collectives, run_sublevel(): decay_total, learn_total = lax.psum((partial_rank, partial_learn), 'head')  31.9 us
    all_gather x2, blocking collectives, run_sublevel(): piece_now = lax.all_gather(lowrank_latent, 'head', axis=2, tiled=True)  24.4 us
    all_gather x2, blocking collectives, run_sublevel(): piece_prev = lax.all_gather(previous, 'head', axis=2, tiled=True)  23.7 us
    unnamed x129, local copies, waits for them, and re-layouts  19.1 us
    dot_general x8, matrix products, sequence_recurrence(): jnp.einsum('rhij,rhj->rhi', states, acceptor_parts[:, position], precisio...  18.2 us
    dot_general x8, matrix products, sequence_recurrence(): jnp.einsum('rhij,rhj->rhi', states, normed[:, position], precision=highest)  16.7 us
    all_to_all x1, starting transfers between devices, body(): lax.all_to_all(outgoing, 'req', split_axis=0, concat_axis=0, tiled=True)  16.6 us
  transfers between devices with their start and end apart: 5, of which 5 were waited for; matrix products, arithmetic and copies ran while one was open for 3% of the time, Pallas kernels for 0%

commit v1 on v0

--- a/solution.py
+++ b/solution.py
@@ -1,9 +1,26 @@
+import functools
 import jax
 import jax.numpy as jnp
 from jax import lax
 from jax.sharding import PartitionSpec as P
 
 highest = lax.Precision.HIGHEST
+
+
+def extend_field(mine, peer_axis):
+    n_axis = lax.axis_size(peer_axis)
+    sides = tuple(((it, (it + 1) % n_axis) for it in range(n_axis)))
+    left_arr, reached = ([mine], [mine])
+    gallery = tuple(((it, (it - 1) % n_axis) for it in range(n_axis)))
+    for _ in range(n_axis // 2):
+        left_arr.append(lax.ppermute(left_arr[-1], peer_axis, sides))
+    for _ in range((n_axis - 1) // 2):
+        reached.append(lax.ppermute(reached[-1], peer_axis, gallery))
+    reply = jnp.concatenate([*left_arr[::-1], *reached[1:]], axis=2)
+    return jnp.roll(reply, (lax.axis_index(peer_axis) - n_axis // 2) * mine.shape[2], axis=2)
+
+
+recover_target_over_axis = functools.partial(extend_field, peer_axis="head")
 
 
 def from_behind(block, axis, distance):
@@ -125,7 +142,7 @@
     batch_rows, steps_count, shard_width = lowrank_latent.shape
     previous = jnp.concatenate([earlier_entry[:, None, :], lowrank_latent[:, :-1, :]], axis=1)
     piece_now = lax.all_gather(lowrank_latent, "head", axis=2, tiled=True)
-    piece_prev = lax.all_gather(previous, "head", axis=2, tiled=True)
+    piece_prev = recover_target_over_axis(previous)
     span_width = piece_now.shape[2]
     coef_rows = lag_interpolants.astype(jnp.float32)
     current_piece = piece_now.astype(jnp.float32)

time: 276 us -> 270 us (0.978)
  blocking collectives: 80 us -> 54.3 us
  starting transfers between devices: 31.3 us -> 50.2 us
  waiting for transfers between devices: 60.6 us -> 63.4 us
    all_gather x2 -> x0, blocking collectives: 23.7 us -> none  [run_sublevel(): piece_prev = lax.all_gather(previous, 'head', axis=2, tiled=True)]
    ppermute x0 -> x6, starting transfers between devices: none -> 18.9 us  [the longest x4 10.1 us: extend_field(): left_arr.append(lax.ppermute(left_arr[-1], peer_axis, sides))]
    unnamed x129 -> x111, local copies, waits for them, and re-layouts: 19.1 us -> 17.1 us
  transfers between devices with their start and end apart: 5 -> 11, of which waited for: 5 -> 5; matrix products, arithmetic and copies ran while one was open for 3% -> 4% of each run, Pallas kernels for 0% -> 0%
where the time goes in v1:
time: 270 us; the launch traced here: 268 us
  waiting for transfers between devices  63.4 us (23%)
  blocking collectives  54.3 us (20%)
  starting transfers between devices  50.2 us (19%)
  matrix products  40.1 us (15%)
  local copies, waits for them, and re-layouts  34 us (13%)
  between operations  14.5 us (5%)
  other arithmetic  11.3 us (4%)
    reduce_scatter x2, waiting for transfers between devices, run_sublevel(): lax.psum_scatter(lax.dot_general(readout_projection, lagged_features, (((...  48.6 us
    psum x2, blocking collectives, run_sublevel(): decay_total, learn_total = lax.psum((partial_rank, partial_learn), 'head')  30.3 us
    all_gather x2, blocking collectives, run_sublevel(): piece_now = lax.all_gather(lowrank_latent, 'head', axis=2, tiled=True)  23.9 us
    dot_general x8, matrix products, sequence_recurrence(): jnp.einsum('rhij,rhj->rhi', states, acceptor_parts[:, position], precisio...  18.2 us
    unnamed x111, local copies, waits for them, and re-layouts  17.1 us
    dot_general x8, matrix products, sequence_recurrence(): jnp.einsum('rhij,rhj->rhi', states, normed[:, position], precision=highest)  16.8 us
    all_to_all x1, starting transfers between devices, body(): lax.all_to_all(outgoing, 'req', split_axis=0, concat_axis=0, tiled=True)  16.6 us
    all_to_all x1, starting transfers between devices, body(): lax.all_to_all(going_back, 'req', split_axis=0, concat_axis=0, tiled=True)  13.3 us
  transfers between devices with their start and end apart: 11, of which 5 were waited for; matrix products, arithmetic and copies ran while one was open for 4% of the time, Pallas kernels for 0%

profile of v1, /device:TPU:8, one launch (start us, length us, event | category | flops | bytes accessed | tf_op | source)
XLA Modules:
  0.0 267.8 jit_solution(7037447072947815110)
XLA Ops:
  6.5 0.9 reshape.364
  8.2 0.7 broadcast.411.clone
  8.9 2.0 scatter_fusion
  10.9 16.6 %all-to-all-start = ((bf16[64,4,256]{2,1,0:T(4,128)(2,1)}), bf16[64,4,256]{2,1,0:T(4,128)(2,1)S(1)}, u32[]{:S(2)}, u32[]{:S(2)}) async-start(bf16[64,4,256]{2,1,0:T(4,128)(2,1)} %scatter_fusion), calls=%async_computation | async-start | bytes 262144 | tf_op jit(solution)/shard_map/all_to_all | solution.py:308
  27.5 0.9 select_reduce_fusion
  30.5 0.8 copy-done.4
  32.9 0.7 add.341
  34.3 0.7 mul.350
  35.6 0.7 mul.354
  36.3 2.8 %all-to-all-done = bf16[64,4,256]{2,1,0:T(4,128)(2,1)S(1)} async-done(((bf16[64,4,256]{2,1,0:T(4,128)(2,1)}), bf16[64,4,256]{2,1,0:T(4,128)(2,1)S(1)}, u32[]{:S(2)}, u32[]{:S(2)}) %all-to-all-start) | async-done | bytes 131104 | tf_op jit(solution)/shard_map/all_to_all | solution.py:308
  40.4 3.4 %collective-permute-start = (bf16[8,4,256]{2,0,1:T(8,128)(2,1)S(1)}, bf16[8,4,256]{2,0,1:T(8,128)(2,1)S(1)}, u32[]{:S(2)}, u32[]{:S(2)}) collective-permute-start(bf16[8,4,256]{2,0,1:T(8,128)(2,1)S(1)} %pad_maximum_fusion.3), channel_id=1, source_target_pairs={{0,1},{1,2},{2,3},{3,0},{4,5},{5,6},{6,7},{7,4},{8,9},{9,10},{10,1... | collective-permute-start | bytes 49160 | tf_op jit(solution)/shard_map/ppermute | solution.py:16
  43.8 3.7 %collective-permute-start.2 = (bf16[8,4,256]{2,0,1:T(8,128)(2,1)S(1)}, bf16[8,4,256]{2,0,1:T(8,128)(2,1)S(1)}, u32[]{:S(2)}, u32[]{:S(2)}) collective-permute-start(bf16[8,4,256]{2,0,1:T(8,128)(2,1)S(1)} %pad_maximum_fusion.3), channel_id=1, source_target_pairs={{0,3},{1,0},{2,1},{3,2},{4,7},{5,4},{6,5},{7,6},{8,11},{9,8},{10,9... | collective-permute-start | bytes 49160 | tf_op jit(solution)/shard_map/ppermute | solution.py:18
  47.6 0.7 copy-done.5
  48.5 0.7 copy-done.6
  49.3 15.9 %all-reduce.1 = (bf16[32,96]{1,0:T(8,128)(2,1)S(1)}, f32[32,96]{1,0:T(8,128)S(1)}) all-reduce(f32[32,96]{1,0:T(8,128)S(1)} %fusion.104, f32[32,96]{1,0:T(8,128)S(1)} %fusion.110), channel_id=1, replica_groups=mesh['section'=2,'req'=64,'head'=4] {'head'}, use_global_device_ids=true, to_apply=%region_6.9 | all-reduce | flops 6144 | bytes 43008 | tf_op jit(solution)/shard_map/psum | solution.py:178
  66.1 0.7 copy-done.45
  67.7 1.9 collective-permute-start.1
  69.6 12.0 %all_gather.6 = bf16[8,4,1024]{2,0,1:T(8,128)(2,1)S(1)} all-gather(bf16[8,4,256]{2,0,1:T(8,128)(2,1)S(1)} %broadcast_select_fusion.1), channel_id=1, replica_groups=mesh['section'=2,'req'=64,'head'=4] {'head'}, dimensions={2}, use_global_device_ids=true | all-gather | bytes 81920 | tf_op jit(solution)/shard_map/all_gather | solution.py:144
  83.7 0.8 broadcast_multiply_fusion.1
  84.5 0.9 reshape.368
  87.0 0.8 reshape.371
  88.3 0.7 copy-done.14
  88.9 1.7 fusion.20
  90.7 2.1 fusion.155
  92.8 0.7 copy-done.22
  93.5 2.1 fusion.180
  95.6 0.7 copy-done.11
  96.3 3.2 %fusion.55 = f32[8,4,1,64]{3,2,1,0:T(1,128)S(1)} fusion(f32[8,4,64]{2,1,0:T(4,128)S(1)} %get-tuple-element.67, f32[8,4,64]{2,1,0:T(4,128)S(1)} %copy.164, f32[8,4,64]{2,1,0:T(4,128)S(1)} %get-tuple-element.27, f32[8,4,64]{2,1,0:T(4,128)S(1)} %bitcast.463, f32[8,4,64]{2,1,0:T(4,128)S(1)} %copy-done.11, f32[8,4,64,1]{2,0,1,3:T(8,128)S(1)} %copy-done.19, ...), kind=kOutput, calls=%fused_computation.72 | convolution fusion | flops 2883584 | bytes 622592 | tf_op jit(solution)/shard_map/rhij,rhj->rhi/dot_general | solution.py:98
  99.5 0.7 copy-done.21
  100.3 2.8 %fusion.54 = f32[8,4,1,64]{3,2,1,0:T(1,128)S(1)} fusion(f32[8,4,64,1]{2,3,1,0:T(1,128)S(1)} %bitcast.473, f32[8,4,64]{2,1,0:T(4,128)S(1)} %get-tuple-element.67, f32[8,4,64]{2,1,0:T(4,128)S(1)} %copy.164, f32[8,4,64]{2,1,0:T(4,128)S(1)} %get-tuple-element.27, f32[8,4,64]{2,1,0:T(4,128)S(1)} %bitcast.464, f32[8,4,64]{2,1,0:T(4,128)S(1)} %copy-done.11, ...), kind=kOutput, calls=%fused_computation.71 | convolution fusion | flops 2883584 | bytes 622592 | tf_op jit(solution)/shard_map/rhij,rhj->rhi/dot_general | solution.py:81
  103.1 0.7 copy-done.10
  103.8 2.0 multiply_add_fusion.2
  105.8 1.7 fusion.152
  107.6 1.7 fusion.190
  109.3 0.7 copy-done.16
  110.1 2.1 fusion.32
  113.6 0.8 convolution_bitcast_fusion.1
  114.5 23.9 %reduce-scatter.3.cloned.1.call-done = f32[256,32]{0,1:T(8,128)} async-done(((f32[1024,32]{0,1:T(8,128)}), f32[256,32]{0,1:T(8,128)}) %reduce-scatter.3.cloned.1.call-update) | async-done | bytes 32784 | tf_op jit(solution)/shard_map/reduce_scatter | solution.py:198
  138.4 0.8 reshape.373
  139.2 1.3 collective-permute-start.3
  140.5 0.8 collective-permute-done.3
  141.4 2.1 collective-permute-start.4
  143.6 5.1 %collective-permute-start.6 = (bf16[8,4,256]{2,0,1:T(8,128)(2,1)S(1)}, bf16[8,4,256]{2,0,1:T(8,128)(2,1)S(1)}, u32[]{:S(2)}, u32[]{:S(2)}) collective-permute-start(bf16[8,4,256]{2,0,1:T(8,128)(2,1)S(1)} %pad_maximum_fusion.2), channel_id=1, source_target_pairs={{0,3},{1,0},{2,1},{3,2},{4,7},{5,4},{6,5},{7,6},{8,11},{9,8},{10,9... | collective-permute-start | bytes 49160 | tf_op jit(solution)/shard_map/ppermute | solution.py:18
  149.0 0.8 copy-done.7
  149.9 14.5 %all-reduce = (bf16[32,96]{1,0:T(8,128)(2,1)S(1)}, f32[32,96]{1,0:T(8,128)S(1)}) all-reduce(f32[32,96]{1,0:T(8,128)S(1)} %fusion.102, f32[32,96]{1,0:T(8,128)S(1)} %fusion.108), channel_id=1, replica_groups=mesh['section'=2,'req'=64,'head'=4] {'head'}, use_global_device_ids=true, to_apply=%region_13.16 | all-reduce | flops 6144 | bytes 43008 | tf_op jit(solution)/shard_map/psum | solution.py:178
  166.2 2.7 collective-permute-start.5
  168.9 11.9 %all_gather.7 = bf16[8,4,1024]{2,0,1:T(8,128)(2,1)S(1)} all-gather(bf16[8,4,256]{2,0,1:T(8,128)(2,1)S(1)} %broadcast_select_fusion), channel_id=1, replica_groups=mesh['section'=2,'req'=64,'head'=4] {'head'}, dimensions={2}, use_global_device_ids=true | all-gather | bytes 81920 | tf_op jit(solution)/shard_map/all_gather | solution.py:144
  183.1 1.7 fusion.18
  185.0 2.1 fusion.149
  187.1 2.1 fusion.175
  189.2 3.2 %fusion.57 = f32[8,4,1,64]{3,2,1,0:T(1,128)S(1)} fusion(f32[8,4,64]{2,1,0:T(4,128)S(1)} %get-tuple-element.47, f32[8,4,64]{2,1,0:T(4,128)S(1)} %copy.178, f32[8,4,64]{2,1,0:T(4,128)S(1)} %get-tuple-element.23, f32[8,4,64]{2,1,0:T(4,128)S(1)} %bitcast.466, f32[8,4,64]{2,1,0:T(4,128)S(1)} %get-tuple-element.35, f32[8,4,64,1]{2,0,1,3:T(8,128)S(1)} %get-tuple-element.32, ...), kind=kOutput, calls=%fused_computation.74 | convolution fusion | flops 2883584 | bytes 622592 | tf_op jit(solution)/shard_map/rhij,rhj->rhi/dot_general | solution.py:98
  192.4 2.8 %fusion.56 = f32[8,4,1,64]{3,2,1,0:T(1,128)S(1)} fusion(f32[8,4,64,1]{2,3,1,0:T(1,128)S(1)} %bitcast.474, f32[8,4,64]{2,1,0:T(4,128)S(1)} %get-tuple-element.47, f32[8,4,64]{2,1,0:T(4,128)S(1)} %copy.178, f32[8,4,64]{2,1,0:T(4,128)S(1)} %get-tuple-element.23, f32[8,4,64]{2,1,0:T(4,128)S(1)} %bitcast.467, f32[8,4,64]{2,1,0:T(4,128)S(1)} %get-tuple-element.35, ...), kind=kOutput, calls=%fused_computation.73 | convolution fusion | flops 2883584 | bytes 622592 | tf_op jit(solution)/shard_map/rhij,rhj->rhi/dot_general | solution.py:81
  195.3 2.0 multiply_add_fusion
  197.3 1.7 fusion.146
  199.0 1.7 fusion.191
  200.8 2.1 fusion.26
  203.6 0.8 convolution_bitcast_fusion
  205.7 0.7 compare_and_fusion
  206.4 24.7 %reduce-scatter.5.cloned.1.call-done = f32[256,32]{0,1:T(8,128)} async-done(((f32[1024,32]{0,1:T(8,128)}), f32[256,32]{0,1:T(8,128)}) %reduce-scatter.5.cloned.1.call-update) | async-done | bytes 32784 | tf_op jit(solution)/shard_map/reduce_scatter | solution.py:198
  231.2 0.8 reshape.382
  232.0 0.7 broadcast.411
  232.7 1.9 scatter_fusion.1
  234.6 13.3 %all-to-all-start.1 = ((bf16[64,4,256]{2,1,0:T(4,128)(2,1)}), bf16[64,4,256]{2,1,0:T(4,128)(2,1)S(1)}, u32[]{:S(2)}, u32[]{:S(2)}) async-start(bf16[64,4,256]{2,1,0:T(4,128)(2,1)} %scatter_fusion.1), calls=%async_computation.3 | async-start | bytes 262144 | tf_op jit(solution)/shard_map/all_to_all | solution.py:314
  248.6 11.1 %all-to-all-done.1 = bf16[64,4,256]{2,1,0:T(4,128)(2,1)S(1)} async-done(((bf16[64,4,256]{2,1,0:T(4,128)(2,1)}), bf16[64,4,256]{2,1,0:T(4,128)(2,1)S(1)}, u32[]{:S(2)}, u32[]{:S(2)}) %all-to-all-start.1) | async-done | bytes 131104 | tf_op jit(solution)/shard_map/all_to_all | solution.py:314
  (228 shorter events, 23.3 us)
Async XLA Ops:
  6.5 107.0 %copy-start = (bf16[1,256,1024]{2,1,0:T(8,128)(2,1)S(1)}, bf16[1,256,1024]{2,1,0:T(8,128)(2,1)}, u32[]{:S(2)}) copy-start(bf16[1,256,1024]{2,1,0:T(8,128)(2,1)} %param.34) | copy-start | bytes 1572868
  6.5 23.8 %copy-start.3 = (bf16[1,1024,256]{2,1,0:T(8,128)(2,1)S(1)}, bf16[1,1024,256]{2,1,0:T(8,128)(2,1)}, u32[]{:S(2)}) copy-start(bf16[1,1024,256]{2,1,0:T(8,128)(2,1)} %param.31) | copy-start | bytes 1572868
  7.4 21.5 %copy-start.9 = (s32[64,8]{1,0:T(8,128)}, s32[64,8]{1,0:T(8,128)S(1)}, u32[]{:S(2)}) copy-start(s32[64,8]{1,0:T(8,128)S(1)} %reshape.364) | copy-start | bytes 6148
  7.6 0.6 copy-start.36
  10.9 28.2 %all-to-all-start = ((bf16[64,4,256]{2,1,0:T(4,128)(2,1)}), bf16[64,4,256]{2,1,0:T(4,128)(2,1)S(1)}, u32[]{:S(2)}, u32[]{:S(2)}) async-start(bf16[64,4,256]{2,1,0:T(4,128)(2,1)} %scatter_fusion), calls=%async_computation | async-start | bytes 262144 | tf_op jit(solution)/shard_map/all_to_all | solution.py:308
  27.5 110.9 %reduce-scatter.3.cloned.1.call-start = ((), (), s32[]{:S(2)}) async-start(), calls=%async_computation.4 | async-start | bytes 163840 | tf_op jit(solution)/shard_map/reduce_scatter | solution.py:198
  29.5 0.8 copy-start.15
  29.7 0.5 copy-start.38
  30.2 17.2 %copy-start.23 = (pred[8]{0:T(512)(128)(4,1)}, pred[8]{0:T(512)(128)(4,1)S(1)}, u32[]{:S(2)}) copy-start(pred[8]{0:T(512)(128)(4,1)S(1)} %get-tuple-element.17) | copy-start | bytes 28
  30.3 17.2 %copy-start.25 = (f32[1,1,256]{2,1,0:T(1,128)}, f32[1,1,256]{2,1,0:T(1,128)S(1)}, u32[]{:S(2)}) copy-start(f32[1,1,256]{2,1,0:T(1,128)S(1)} %get-tuple-element.82) | copy-start | bytes 3076
  30.3 17.2 %copy-start.27 = (f32[1,1,256]{2,1,0:T(1,128)}, f32[1,1,256]{2,1,0:T(1,128)S(1)}, u32[]{:S(2)}) copy-start(f32[1,1,256]{2,1,0:T(1,128)S(1)} %get-tuple-element.83) | copy-start | bytes 3076
  30.3 1.0 copy-start.4
  31.6 0.7 copy-start.40
  32.9 0.7 copy-start.41
  34.3 0.7 copy-start.42
  39.7 0.7 copy-start.8
  40.4 27.4 %collective-permute-start = (bf16[8,4,256]{2,0,1:T(8,128)(2,1)S(1)}, bf16[8,4,256]{2,0,1:T(8,128)(2,1)S(1)}, u32[]{:S(2)}, u32[]{:S(2)}) collective-permute-start(bf16[8,4,256]{2,0,1:T(8,128)(2,1)S(1)} %pad_maximum_fusion.3), channel_id=1, source_target_pairs={{0,1},{1,2},{2,3},{3,0},{4,5},{5,6},{6,7},{7,4},{8,9},{9,10},{10,1... | collective-permute-start | bytes 49160 | tf_op jit(solution)/shard_map/ppermute | solution.py:16
  43.8 37.9 %collective-permute-start.2 = (bf16[8,4,256]{2,0,1:T(8,128)(2,1)S(1)}, bf16[8,4,256]{2,0,1:T(8,128)(2,1)S(1)}, u32[]{:S(2)}, u32[]{:S(2)}) collective-permute-start(bf16[8,4,256]{2,0,1:T(8,128)(2,1)S(1)} %pad_maximum_fusion.3), channel_id=1, source_target_pairs={{0,3},{1,0},{2,1},{3,2},{4,7},{5,4},{6,5},{7,6},{8,11},{9,8},{10,9... | collective-permute-start | bytes 49160 | tf_op jit(solution)/shard_map/ppermute | solution.py:18
  47.5 0.8 copy-start.5
  48.4 0.8 copy-start.6
  49.1 16.0 %copy-start.47 = (bf16[1,96,256]{2,1,0:T(8,128)(2,1)S(1)}, bf16[1,96,256]{2,1,0:T(8,128)(2,1)}, u32[]{:S(2)}) copy-start(bf16[1,96,256]{2,1,0:T(8,128)(2,1)} %param.36) | copy-start | bytes 147460
  65.2 0.7 copy-start.51
  66.0 0.8 copy-start.45
  66.1 0.7 copy-start.49
  67.7 14.0 %collective-permute-start.1 = (bf16[8,4,256]{2,0,1:T(8,128)(2,1)S(1)}, bf16[8,4,256]{2,0,1:T(8,128)(2,1)S(1)}, u32[]{:S(2)}, u32[]{:S(2)}) collective-permute-start(bf16[8,4,256]{2,0,1:T(8,128)(2,1)S(1)} %collective-permute-done), channel_id=1, source_target_pairs={{0,1},{1,2},{2,3},{3,0},{4,5},{5,6},{6,7},{7,4},{8,9},{9,10},{10,1... | collective-permute-start | bytes 49160 | tf_op jit(solution)/shard_map/ppermute | solution.py:16
  81.9 1.1 copy-start.2
  83.0 0.7 copy-start.31
  83.0 0.7 copy-start.29
  84.5 3.7 %copy-start.1 = (f32[1,8,4,64,64]{4,3,2,1,0:T(8,128)S(1)}, f32[1,8,4,64,64]{4,3,2,1,0:T(8,128)}, u32[]{:S(2)}) copy-start(f32[1,8,4,64,64]{4,3,2,1,0:T(8,128)} %param.28) | copy-start | bytes 1572868
  88.2 0.7 copy-start.14
  88.9 1.7 copy-start.12
  88.9 1.7 copy-start.20
  92.8 0.7 copy-start.22
  95.6 0.7 copy-start.11
  95.6 0.7 copy-start.19
  99.5 0.7 copy-start.21
  103.1 0.7 copy-start.10
  103.8 2.0 copy-start.13
  107.6 1.8 copy-start.18
  109.3 0.7 copy-start.16
  109.3 0.7 copy-start.17
  112.4 0.7 copy-start.33
  112.4 0.7 copy-start.34
  112.5 0.7 copy-start.35
  114.4 116.8 %reduce-scatter.5.cloned.1.call-start = ((), (), s32[]{:S(2)}) async-start(), calls=%async_computation.5 | async-start | bytes 163840 | tf_op jit(solution)/shard_map/reduce_scatter | solution.py:198
  138.4 0.8 copy-start.24
  139.2 2.1 collective-permute-start.3
  141.4 7.3 %copy-start.26 = (f32[1,1,256]{2,1,0:T(1,128)S(1)}, f32[1,1,256]{2,1,0:T(1,128)}, u32[]{:S(2)}) copy-start(f32[1,1,256]{2,1,0:T(1,128)} %copy-done.25) | copy-start | bytes 3076
  141.4 7.3 %copy-start.28 = (f32[1,1,256]{2,1,0:T(1,128)S(1)}, f32[1,1,256]{2,1,0:T(1,128)}, u32[]{:S(2)}) copy-start(f32[1,1,256]{2,1,0:T(1,128)} %copy-done.27) | copy-start | bytes 3076
  141.4 24.8 %collective-permute-start.4 = (bf16[8,4,256]{2,0,1:T(8,128)(2,1)S(1)}, bf16[8,4,256]{2,0,1:T(8,128)(2,1)S(1)}, u32[]{:S(2)}, u32[]{:S(2)}) collective-permute-start(bf16[8,4,256]{2,0,1:T(8,128)(2,1)S(1)} %pad_maximum_fusion.2), channel_id=1, source_target_pairs={{0,1},{1,2},{2,3},{3,0},{4,5},{5,6},{6,7},{7,4},{8,9},{9,10},{10,1... | collective-permute-start | bytes 49160 | tf_op jit(solution)/shard_map/ppermute | solution.py:16
  143.6 37.2 %collective-permute-start.6 = (bf16[8,4,256]{2,0,1:T(8,128)(2,1)S(1)}, bf16[8,4,256]{2,0,1:T(8,128)(2,1)S(1)}, u32[]{:S(2)}, u32[]{:S(2)}) collective-permute-start(bf16[8,4,256]{2,0,1:T(8,128)(2,1)S(1)} %pad_maximum_fusion.2), channel_id=1, source_target_pairs={{0,3},{1,0},{2,1},{3,2},{4,7},{5,4},{6,5},{7,6},{8,11},{9,8},{10,9... | collective-permute-start | bytes 49160 | tf_op jit(solution)/shard_map/ppermute | solution.py:18
  148.9 0.8 copy-start.7
  149.7 14.6 %copy-start.46 = (bf16[1,96,256]{2,1,0:T(8,128)(2,1)S(1)}, bf16[1,96,256]{2,1,0:T(8,128)(2,1)}, u32[]{:S(2)}) copy-start(bf16[1,96,256]{2,1,0:T(8,128)(2,1)} %param.38) | copy-start | bytes 147460
  164.3 0.7 copy-start.50
  165.0 0.8 copy-start.48
  165.2 0.7 copy-start.52
  166.2 14.5 %collective-permute-start.5 = (bf16[8,4,256]{2,0,1:T(8,128)(2,1)S(1)}, bf16[8,4,256]{2,0,1:T(8,128)(2,1)S(1)}, u32[]{:S(2)}, u32[]{:S(2)}) collective-permute-start(bf16[8,4,256]{2,0,1:T(8,128)(2,1)S(1)} %collective-permute-done.4), channel_id=1, source_target_pairs={{0,1},{1,2},{2,3},{3,0},{4,5},{5,6},{6,7},{7,4},{8,9},{9,10},{10,1... | collective-permute-start | bytes 49160 | tf_op jit(solution)/shard_map/ppermute | solution.py:16
  181.8 0.7 copy-start.30
  181.8 0.7 copy-start.32
  204.5 0.6 copy-start.39
  204.5 0.6 copy-start.44
  205.1 0.7 copy-start.37
  234.6 25.1 %all-to-all-start.1 = ((bf16[64,4,256]{2,1,0:T(4,128)(2,1)}), bf16[64,4,256]{2,1,0:T(4,128)(2,1)S(1)}, u32[]{:S(2)}, u32[]{:S(2)}) async-start(bf16[64,4,256]{2,1,0:T(4,128)(2,1)} %scatter_fusion.1), calls=%async_computation.3 | async-start | bytes 262144 | tf_op jit(solution)/shard_map/all_to_all | solution.py:314
  247.9 0.7 copy-start.53
  (1 other events, 0.5 us)
Sparse Core Ops, SparseCore 0:
  114.5 23.7 reduce-scatter.2
  204.6 26.5 reduce-scatter.4
